TPU v7x, 128 devices: a whole 4x4x4 slice. The times are simulated.
128 devices in a mesh: req: 2 (over core), seq: 64 (over z, y, x).
Axes of the slice: x: 4, y: 4, z: 4, core: 2. Of those that a mesh axis runs over, the one named last changes fastest.
Arguments:
- tokens: bfloat16 [4, 128, 1536], P(None, ('req', 'seq')), may hold values from -6 to 6
- lengths: int32 [128], P('req'), may hold values from 1 to 16384, as said below
- k_cache: bfloat16 [128, 4096, 256], P('req', 'seq'), may hold values from -500 to 500
- v_cache: bfloat16 [128, 4096, 256], P('req', 'seq'), may hold values from -12 to 12
- attn_gain: bfloat16 [1536], replicated, may hold values from 0.5 to 1.5
- w_qkv: bfloat16 [1536, 2048], replicated, may hold values from -0.15625 to 0.15625
- sink: float32 [12], replicated, may hold values from -1 to 3
- w_out: bfloat16 [1536, 1536], replicated, may hold values from -0.15625 to 0.15625
- moe_gain: bfloat16 [1536], replicated, may hold values from 0.5 to 1.5
- router: bfloat16 [1536, 32], replicated, may hold values from -0.15625 to 0.15625
- w_gate: bfloat16 [1536, 24576], P(None, ('req', 'seq')), may hold values from -0.15625 to 0.15625
- w_up: bfloat16 [1536, 24576], P(None, ('req', 'seq')), may hold values from -0.15625 to 0.15625
- w_down: bfloat16 [24576, 1536], P(('req', 'seq')), may hold values from -0.21875 to 0.21875
- routes: int32 [128, 4, 4], replicated, may hold values from 0 to 31, all different within a row; in each aligned block of 4 rows (0 to 3, 4 to 7, ..., all dimensions but the last counted through in order) at most 2 rows name the same one
Outputs:
- outputs: bfloat16 [4, 128, 1536], P(None, ('req', 'seq'))
Inputs may be any that keep to these rules, and one draw needn't show every extreme that they name: Each request has lengths positions before the first step; some request has all 16384 in every draw. `routes`: among the 4 tokens of one device's requests (requests 1 d .. 1 d + 1 - 1, all steps), no expert is named by more than 2 tokens, and in every draw some expert is named by exactly 2.
All inputs are finite; a program needn't handle non-finite values.
Results may differ from a plain program's by a relative error of at most 0.02.
Values may be sent and summed in bfloat16 or wider, within the bound.
No kernel may reach another device: no remote copies, remote signals or barrier semaphores. Data moves between devices by JAX's collectives and lax.ppermute only.
A program may use at most 512 MiB of HBM per device.

v0:
```python
import jax
import jax.numpy as jnp
from jax import lax
from jax.sharding import PartitionSpec as P

D = 1536
QH = 12
KVH = 2
HD = 128
E = 32
EFF = 768
TOP = 4
STEPS = 4
MOST = 2


def combined_all(value, axis, join):
    gathered = jax.tree.map(
        lambda a, kind: lax.all_gather(a.astype(kind), axis),
        value,
        (jnp.bfloat16, jnp.bfloat16, jnp.bfloat16),
    )

    def take(source):
        return jax.tree.map(
            lambda a, own: lax.dynamic_index_in_dim(a, source, 0, False).astype(own.dtype),
            gathered,
            value,
        )

    return lax.fori_loop(
        1, lax.axis_size(axis), lambda source, state: join(state, take(source)), take(0)
    )


def normalize(x, gain):
    xf = x.astype(jnp.float32)
    inv = lax.rsqrt(jnp.mean(xf * xf, axis=-1, keepdims=True) + 1e-05)
    return (xf * inv * gain.astype(jnp.float32)).astype(jnp.bfloat16)


def rotate(x, place):
    half = x.shape[-1] // 2
    index = jnp.arange(half, dtype=jnp.float32)
    inverse = jnp.exp(-jnp.log(1000000.0) * 2.0 * index / x.shape[-1])
    angle = place.astype(jnp.float32)[..., None, None] * inverse
    first = x[..., :half]
    second = x[..., half:]
    cosine = jnp.cos(angle)
    sine = jnp.sin(angle)
    return jnp.concatenate(
        [first * cosine - second * sine, second * cosine + first * sine], axis=-1
    )


def route_weights(logits, picks):
    onehot = (picks[:, :, None] == jnp.arange(E, dtype=jnp.int32)[None, None, :]).astype(
        jnp.float32
    )
    chosen = jnp.sum(onehot * logits[:, None, :], axis=-1)
    share = jax.nn.softmax(chosen, axis=-1)
    return jnp.sum(share[:, :, None] * onehot, axis=1)


def combine_parts(first, second):
    peak = jnp.maximum(first[0], second[0])
    left_scale = jnp.exp(first[0] - peak)
    right_scale = jnp.exp(second[0] - peak)
    return (
        peak,
        first[1] * left_scale + second[1] * right_scale,
        first[2] * left_scale[..., None] + second[2] * right_scale[..., None],
    )


def on_device(
    tokens,
    lengths,
    k_cache,
    v_cache,
    attn_gain,
    w_qkv,
    sink,
    w_out,
    moe_gain,
    router,
    w_gate,
    w_up,
    w_down,
    routes,
):
    seq_count = lax.axis_size("seq")
    seq_place = lax.axis_index("seq")
    device = lax.axis_index("req") * seq_count + seq_place
    devices = lax.axis_size(("req", "seq"))
    rows = tokens.shape[1]
    group_rows = lengths.shape[0]
    local_pos = k_cache.shape[1]
    window = local_pos * seq_count
    heads_per = QH // KVH
    scale = HD ** (-0.5)
    columns = w_gate.shape[1]
    expert_mine = device * columns // EFF
    own_len = lax.dynamic_slice_in_dim(lengths, seq_place * rows, rows)
    step_ids = jnp.arange(STEPS, dtype=jnp.int32)
    a = normalize(tokens, attn_gain)
    proj = jnp.einsum("srm,mn->srn", a, w_qkv, preferred_element_type=jnp.float32)
    place = own_len[None, :] + step_ids[:, None]
    query = rotate(proj[..., : QH * HD].reshape(STEPS, rows, QH, HD), place).astype(jnp.bfloat16)
    fresh_key = rotate(
        proj[..., QH * HD : (QH + KVH) * HD].reshape(STEPS, rows, KVH, HD), place
    ).astype(jnp.bfloat16)
    fresh_val = proj[..., (QH + KVH) * HD :].reshape(STEPS, rows, KVH, HD).astype(jnp.bfloat16)
    every_query = lax.all_gather(query.reshape(STEPS, rows, QH * HD), "seq", axis=1, tiled=True)
    grouped_all = every_query.reshape(STEPS, group_rows, KVH, heads_per, HD)
    cache_keys = k_cache.reshape(group_rows, local_pos, KVH, HD)
    cache_vals = v_cache.reshape(group_rows, local_pos, KVH, HD)
    scores = (
        jnp.einsum("tnkgd,nckd->tnkgc", grouped_all, cache_keys, preferred_element_type=jnp.float32)
        * scale
    )
    key_slot = seq_place * local_pos + jnp.arange(local_pos, dtype=jnp.int32)
    back = jnp.mod(lengths[None, :, None] - 1 - key_slot[None, None, :], window)
    reach = jnp.minimum(lengths[None, :, None], window - 1 - step_ids[:, None, None])
    valid = (back < reach)[:, :, None, None, :]
    peak_local = jnp.max(jnp.where(valid, scores, -1e30), axis=-1)
    weights = jnp.where(valid, jnp.exp(scores - peak_local[..., None]), 0.0)
    total_local = jnp.sum(weights, axis=-1)
    mixed_local = jnp.einsum(
        "tnkgc,nckd->tnkgd",
        weights.astype(jnp.bfloat16),
        cache_vals,
        preferred_element_type=jnp.float32,
    )
    peak_all, total_all, mixed_all = combined_all(
        (peak_local, total_local, mixed_local), "seq", combine_parts
    )
    peak = lax.dynamic_slice_in_dim(peak_all, seq_place * rows, rows, 1)
    total = lax.dynamic_slice_in_dim(total_all, seq_place * rows, rows, 1)
    mixed = lax.dynamic_slice_in_dim(mixed_all, seq_place * rows, rows, 1)
    grouped = query.reshape(STEPS, rows, KVH, heads_per, HD)
    tail_scores = (
        jnp.einsum("trkgd,srkd->trkgs", grouped, fresh_key, preferred_element_type=jnp.float32)
        * scale
    )
    tail_valid = (step_ids[None, :] <= step_ids[:, None])[:, None, None, None, :]
    sink_grid = sink.reshape(KVH, heads_per)[None, None]
    final = jnp.maximum(
        jnp.maximum(peak, jnp.max(jnp.where(tail_valid, tail_scores, -1e30), axis=-1)), sink_grid
    )
    shift = jnp.exp(peak - final)
    tail_w = jnp.where(tail_valid, jnp.exp(tail_scores - final[..., None]), 0.0)
    denom = total * shift + jnp.sum(tail_w, axis=-1) + jnp.exp(sink_grid - final)
    mixed = mixed * shift[..., None] + jnp.einsum(
        "trkgs,srkd->trkgd",
        tail_w.astype(jnp.bfloat16),
        fresh_val,
        preferred_element_type=jnp.float32,
    )
    attn = (mixed / denom[..., None]).reshape(STEPS, rows, QH * HD).astype(jnp.bfloat16)
    h = (
        tokens.astype(jnp.float32)
        + jnp.einsum("srn,nm->srm", attn, w_out, preferred_element_type=jnp.float32)
    ).astype(jnp.bfloat16)
    u = normalize(h, moe_gain)
    own_tokens = rows * STEPS
    u_tok = u.transpose(1, 0, 2).reshape(own_tokens, D)
    every_row = lax.all_gather(u_tok, ("req", "seq"), axis=0, tiled=True)
    all_picks = routes.reshape(-1, TOP)
    every_logit = jnp.dot(every_row, router, preferred_element_type=jnp.float32)
    dense_all = route_weights(every_logit, all_picks)
    weight_mine = jnp.sum(
        dense_all * (jnp.arange(E, dtype=jnp.int32) == expert_mine)[None, :].astype(jnp.float32),
        axis=-1,
    )
    mine = jnp.any(all_picks == expert_mine, axis=-1)
    slot = jnp.cumsum(mine.astype(jnp.int32)) - 1
    limit = MOST * devices
    select = (
        (slot[None, :] == jnp.arange(limit, dtype=jnp.int32)[:, None]) & mine[None, :]
    ).astype(jnp.float32)
    picked = jnp.dot(
        select.astype(jnp.bfloat16), every_row, preferred_element_type=jnp.float32
    ).astype(jnp.bfloat16)
    slot_weight = jnp.dot(select, weight_mine, precision=lax.Precision.HIGHEST)
    hidden = (
        jax.nn.relu(jnp.dot(picked, w_gate, preferred_element_type=jnp.float32))
        * jnp.dot(picked, w_up, preferred_element_type=jnp.float32)
    ).astype(jnp.bfloat16)
    produced = jnp.dot(hidden, w_down, preferred_element_type=jnp.float32) * slot_weight[:, None]
    moe = lax.psum_scatter(
        jnp.einsum("lc,lm->cm", select, produced, precision=lax.Precision.HIGHEST),
        ("req", "seq"),
        scatter_dimension=0,
        tiled=True,
    )
    moe_steps = moe.reshape(rows, STEPS, D).transpose(1, 0, 2)
    return (h.astype(jnp.float32) + moe_steps).astype(jnp.bfloat16)


def solution(mesh):
    in_specs = (
        P(None, ("req", "seq"), None),
        P("req"),
        P("req", "seq", None),
        P("req", "seq", None),
        P(),
        P(),
        P(),
        P(),
        P(),
        P(),
        P(None, ("req", "seq")),
        P(None, ("req", "seq")),
        P(("req", "seq"), None),
        P(),
    )
    out_specs = P(None, ("req", "seq"), None)
    return jax.shard_map(
        on_device, mesh=mesh, in_specs=in_specs, out_specs=out_specs, check_vma=False
    )
```

profile of v0, /device:TPU:1, one launch (start us, length us, event | category | flops | bytes accessed | tf_op | source)
XLA Modules:
  0.0 1043.7 jit_solution(8082044500679967716)
XLA Ops:
  8.2 3.9 convolution_bitcast_fusion.1
  17.0 155.1 %all_gather.20 = bf16[4,64,1536]{2,0,1:T(4,128)(2,1)S(1)} all-gather(bf16[4,1,1536]{2,0,1:T(4,128)(2,1)S(1)} %convert_element_type.198), channel_id=1, replica_groups=mesh['req'=2,'seq'=64] {'seq'}, dimensions={1}, use_global_device_ids=true | all-gather | bytes 798720 | tf_op jit(solution)/shard_map/all_gather | solution.py:114
  175.9 3.4 fusion.8
  184.5 149.0 %all-gather = bf16[256,64,2,6]{1,2,3,0:T(2,128)(2,1)S(1)} all-gather(bf16[4,64,2,6]{1,2,3,0:T(2,128)(2,1)S(1)} %copy.158), channel_id=2, replica_groups=mesh['req'=2,'seq'=64] {'seq'}, dimensions={0}, use_global_device_ids=true | all-gather | bytes 399360 | tf_op jit(solution)/shard_map/all_gather | solution.py:19
  333.5 156.4 %all-gather.1 = bf16[256,64,2,6]{1,2,3,0:T(2,128)(2,1)S(1)} all-gather(bf16[4,64,2,6]{1,2,3,0:T(2,128)(2,1)S(1)} %copy.160), channel_id=3, replica_groups=mesh['req'=2,'seq'=64] {'seq'}, dimensions={0}, use_global_device_ids=true | all-gather | bytes 399360 | tf_op jit(solution)/shard_map/all_gather | solution.py:19
  490.9 40.0 %all-gather.7.cloned.1.call-done = bf16[256,64,2,6,128]{4,3,0,2,1:T(8,128)(2,1)} async-done(((bf16[4,64,2,6,128]{4,3,0,2,1:T(8,128)(2,1)}), bf16[256,64,2,6,128]{4,3,0,2,1:T(8,128)(2,1)}) %all-gather.7.cloned.1.call-update) | async-done | bytes 50331664 | tf_op jit(solution)/shard_map/all_gather | solution.py:19
  532.5 233.8 %while.19 = (s32[]{:T(128)}, f32[4,64,2,6]{1,2,3,0:T(2,128)S(1)}, f32[4,64,2,6]{1,2,3,0:T(2,128)S(1)}, f32[4,64,2,6,128]{4,3,2,1,0:T(8,128)S(1)}, bf16[64,4,64,2...) while((s32[]{:T(128)}, f32[4,64,2,6]{1,2,3,0:T(2,128)S(1)}, ...), condition=%wide.region_4.5_spmd, body=%wide.region_3.4_spmd.sunk | while | flops 1597445 | bytes 4354199 | solution.py:31
  533.7 2.5 fusion.101
  537.4 2.5 fusion.101
  541.1 2.5 fusion.101
  544.9 2.5 fusion.101
  548.6 2.5 fusion.101
  552.3 2.5 fusion.101
  556.0 2.5 fusion.101
  559.7 2.5 fusion.101
  563.4 2.5 fusion.101
  567.1 2.5 fusion.101
  570.8 2.5 fusion.101
  574.6 2.5 fusion.101
  578.3 2.5 fusion.101
  582.0 2.5 fusion.101
  585.7 2.5 fusion.101
  589.4 2.5 fusion.101
  593.1 2.5 fusion.101
  596.8 2.5 fusion.101
  600.5 2.5 fusion.101
  604.2 2.5 fusion.101
  608.0 2.5 fusion.101
  611.7 2.5 fusion.101
  615.4 2.5 fusion.101
  619.1 2.5 fusion.101
  622.8 2.5 fusion.101
  626.5 2.5 fusion.101
  630.2 2.5 fusion.101
  633.9 2.5 fusion.101
  637.7 2.5 fusion.101
  641.4 2.5 fusion.101
  645.1 2.5 fusion.101
  648.8 2.5 fusion.101
  652.5 2.5 fusion.101
  656.2 2.5 fusion.101
  659.9 2.5 fusion.101
  663.6 2.5 fusion.101
  689.6 2.5 fusion.101
  768.0 3.2 multiply_reduce_fusion.1
  773.7 100.2 %all-gather.9.cloned.1.call-done = bf16[512,1,1536]{2,1,0:T(2,128)(2,1)} async-done(((bf16[4,1,1536]{2,1,0:T(2,128)(2,1)}), bf16[512,1,1536]{2,1,0:T(2,128)(2,1)}) %all-gather.9.cloned.1.call-update) | async-done | bytes 1572880 | tf_op jit(solution)/shard_map/all_gather | solution.py:168
  882.2 3.3 fusion.38
  885.5 150.3 %all-reduce.3.cloned.1.call-done = f32[512,1536]{1,0:T(8,128)} async-done(((f32[512,1536]{1,0:T(8,128)}), f32[512,1536]{1,0:T(8,128)}) %all-reduce.3.cloned.1.call-update) | async-done | bytes 3145744
  (331 shorter events, 169.6 us)
Async XLA Ops:
  6.5 873.4 %copy-start = (bf16[192,1536]{1,0:T(8,128)(2,1)S(1)}, bf16[192,1536]{1,0:T(8,128)(2,1)}, u32[]{:S(2)}) copy-start(bf16[192,1536]{1,0:T(8,128)(2,1)} %param.28) | copy-start | bytes 1769476
  6.5 524.3 %all-gather.7.cloned.1.call-start = ((), (), s32[]{:S(2)}) async-start(), calls=%async_computation | async-start | bytes 68157440 | tf_op jit(solution)/shard_map/all_gather | solution.py:19
  8.2 4.6 copy-start.12
  8.2 6.5 copy-start.1
  12.1 0.6 copy-start.8
  16.7 156.9 %copy-start.2 = (bf16[64,64,256]{2,1,0:T(8,128)(2,1)S(1)}, bf16[64,64,256]{2,1,0:T(8,128)(2,1)}, u32[]{:S(2)}) copy-start(bf16[64,64,256]{2,1,0:T(8,128)(2,1)} %param.19) | copy-start | bytes 6291460
  173.6 2.1 copy-start.7
  175.9 3.4 copy-start.3
  181.4 1.9 copy-start.14
  181.4 2.0 copy-start.11
  181.5 692.5 %all-gather.9.cloned.1.call-start = ((), (), s32[]{:S(2)}) async-start(), calls=%async_computation.1 | async-start | bytes 3170304 | tf_op jit(solution)/shard_map/all_gather | solution.py:168
  333.5 156.5 %copy-start.4 = (bf16[256,64,2,6]{1,2,3,0:T(2,128)(2,1)}, bf16[256,64,2,6]{1,2,3,0:T(2,128)(2,1)S(1)}, u32[]{:S(2)}) copy-start(bf16[256,64,2,6]{1,2,3,0:T(2,128)(2,1)S(1)} %all-gather) | copy-start | bytes 1179652
  489.9 0.9 copy-start.5
  532.5 235.5 %copy-start.9 = (bf16[4,1,1536]{2,0,1:T(4,128)(2,1)S(1)}, bf16[4,1,1536]{2,0,1:T(4,128)(2,1)}, u32[]{:S(2)}) copy-start(bf16[4,1,1536]{2,0,1:T(4,128)(2,1)} %param.16) | copy-start | bytes 36868
  768.0 4.2 copy-start.10
  768.0 105.9 %copy-start.13 = (bf16[1536,32]{0,1:T(8,128)(2,1)S(1)}, bf16[1536,32]{0,1:T(8,128)(2,1)}, u32[]{:S(2)}) copy-start(bf16[1536,32]{0,1:T(8,128)(2,1)} %param.25) | copy-start | bytes 294916
  772.0 263.8 %all-reduce.3.cloned.1.call-start = ((), (), s32[]{:S(2)}) async-start(), calls=%async_computation.2 | async-start | bytes 6291456
  876.4 3.1 copy-start.6
Sparse Core Ops, SparseCore 0:
  181.6 349.2 all-gather.6
  772.1 101.7 all-gather.8
  885.6 150.1 all-reduce.2
where the time goes:
time: 1050 us; the launch traced here: 1040 us
  blocking collectives  461 us (44%)
  waiting for transfers between devices  291 us (28%)
  other arithmetic  218 us (21%)
  local copies, waits for them, and re-layouts  33.8 us (3%)
  matrix products  25 us (2%)
  between operations  13.6 us (1%)
    all_gather x2, blocking collectives, combined_all(): lax.all_gather(a.astype(kind), axis)  305 us
    add x63, other arithmetic, combine_parts(): first[2] * left_scale[..., None] + second[2] * right_scale[..., None]  159 us
    all_gather x1, blocking collectives, on_device(): lax.all_gather(query.reshape(STEPS, rows, QH * HD), 'seq', axis=1, tiled=...  155 us
    unnamed x4, waiting for transfers between devices  150 us
    all_gather x1, waiting for transfers between devices, on_device(): every_row = lax.all_gather(u_tok, ('req', 'seq'), axis=0, tiled=True)  100 us
    add x63, other arithmetic, combine_parts(): first[1] * left_scale + second[1] * right_scale  49.8 us
    all_gather x1, waiting for transfers between devices, combined_all(): lax.all_gather(a.astype(kind), axis)  40 us
  transfers between devices with their start and end apart: 3, of which 3 were waited for; matrix products, arithmetic and copies ran while one was open for 0% of the time, Pallas kernels for 0%

commit v1 on v0

--- a/solution.py
+++ b/solution.py
@@ -12,6 +12,12 @@
 TOP = 4
 STEPS = 4
 MOST = 2
+
+
+def tiled_gather(x, axis, dim):
+    devices = lax.axis_size(axis)
+    repeats = [devices if d == dim else 1 for d in range(x.ndim)]
+    return lax.all_to_all(jnp.tile(x, repeats), axis, split_axis=dim, concat_axis=dim, tiled=True)
 
 
 def combined_all(value, axis, join):
@@ -111,7 +117,7 @@
         proj[..., QH * HD : (QH + KVH) * HD].reshape(STEPS, rows, KVH, HD), place
     ).astype(jnp.bfloat16)
     fresh_val = proj[..., (QH + KVH) * HD :].reshape(STEPS, rows, KVH, HD).astype(jnp.bfloat16)
-    every_query = lax.all_gather(query.reshape(STEPS, rows, QH * HD), "seq", axis=1, tiled=True)
+    every_query = tiled_gather(query.reshape(STEPS, rows, QH * HD), "seq", 1)
     grouped_all = every_query.reshape(STEPS, group_rows, KVH, heads_per, HD)
     cache_keys = k_cache.reshape(group_rows, local_pos, KVH, HD)
     cache_vals = v_cache.reshape(group_rows, local_pos, KVH, HD)

time: 1050 us -> 894 us (0.85)
  blocking collectives: 461 us -> 307 us
  waiting for transfers between devices: 291 us -> 272 us
  starting transfers between devices: 0.27 us -> 12.3 us
    all_gather x1 -> x0, blocking collectives: 155 us -> none  [on_device(): lax.all_gather(query.reshape(STEPS, rows, QH * HD), 'seq', axis=1, tiled=...]
    all_gather x1, waiting for transfers between devices: 40 us -> 17.2 us  [combined_all(): lax.all_gather(a.astype(kind), axis)]
    all_to_all x0 -> x1, starting transfers between devices: none -> 12 us  [tiled_gather(): lax.all_to_all(jnp.tile(x, repeats), axis, split_axis=dim, concat_axis=di...]
  transfers between devices with their start and end apart: 3 -> 4, of which waited for: 3 -> 4; matrix products, arithmetic and copies ran while one was open for 0% -> 1% of each run, Pallas kernels for 0% -> 0%
where the time goes in v1:
time: 894 us; the launch traced here: 884 us
  blocking collectives  307 us (34%)
  waiting for transfers between devices  272 us (30%)
  other arithmetic  218 us (24%)
  local copies, waits for them, and re-layouts  35.6 us (4%)
  matrix products  24.2 us (3%)
  between operations  13.6 us (2%)
  starting transfers between devices  12.3 us (1%)
    all_gather x2, blocking collectives, combined_all(): lax.all_gather(a.astype(kind), axis)  307 us
    add x63, other arithmetic, combine_parts(): first[2] * left_scale[..., None] + second[2] * right_scale[..., None]  159 us
    unnamed x4, waiting for transfers between devices  150 us
    all_gather x1, waiting for transfers between devices, on_device(): every_row = lax.all_gather(u_tok, ('req', 'seq'), axis=0, tiled=True)  96.3 us
    add x63, other arithmetic, combine_parts(): first[1] * left_scale + second[1] * right_scale  49.8 us
  transfers between devices with their start and end apart: 4, of which 4 were waited for; matrix products, arithmetic and copies ran while one was open for 1% of the time, Pallas kernels for 0%

profile of v1, /device:TPU:1, one launch (start us, length us, event | category | flops | bytes accessed | tf_op | source)
XLA Modules:
  0.0 884.0 jit_solution(559090187998053290)
XLA Ops:
  8.2 3.8 convolution_bitcast_fusion.1
  14.6 12.0 %all-to-all-start = ((bf16[4,64,1536]{2,0,1:T(4,128)(2,1)}), bf16[4,64,1536]{2,0,1:T(4,128)(2,1)S(1)}, u32[]{:S(2)}, u32[]{:S(2)}) async-start(bf16[4,64,1536]{2,0,1:T(4,128)(2,1)} %tile.2), calls=%async_computation | async-start | bytes 1572864 | tf_op jit(solution)/shard_map/all_to_all | solution.py:20
  29.2 4.0 reshape.422
  33.5 8.0 all-to-all-done
  43.0 3.4 fusion.8
  51.0 151.7 %all-gather = bf16[256,64,2,6]{1,2,3,0:T(2,128)(2,1)S(1)} all-gather(bf16[4,64,2,6]{1,2,3,0:T(2,128)(2,1)S(1)} %copy.157), channel_id=2, replica_groups=mesh['req'=2,'seq'=64] {'seq'}, dimensions={0}, use_global_device_ids=true | all-gather | bytes 399360 | tf_op jit(solution)/shard_map/all_gather | solution.py:25
  202.7 155.0 %all-gather.1 = bf16[256,64,2,6]{1,2,3,0:T(2,128)(2,1)S(1)} all-gather(bf16[4,64,2,6]{1,2,3,0:T(2,128)(2,1)S(1)} %copy.159), channel_id=3, replica_groups=mesh['req'=2,'seq'=64] {'seq'}, dimensions={0}, use_global_device_ids=true | all-gather | bytes 399360 | tf_op jit(solution)/shard_map/all_gather | solution.py:25
  358.6 17.2 %all-gather.7.cloned.1.call-done = bf16[256,64,2,6,128]{4,3,0,2,1:T(8,128)(2,1)} async-done(((bf16[4,64,2,6,128]{4,3,0,2,1:T(8,128)(2,1)}), bf16[256,64,2,6,128]{4,3,0,2,1:T(8,128)(2,1)}) %all-gather.7.cloned.1.call-update) | async-done | bytes 50331664 | tf_op jit(solution)/shard_map/all_gather | solution.py:25
  377.4 233.8 %while.19 = (s32[]{:T(128)}, f32[4,64,2,6]{1,2,3,0:T(2,128)S(1)}, f32[4,64,2,6]{1,2,3,0:T(2,128)S(1)}, f32[4,64,2,6,128]{4,3,2,1,0:T(8,128)S(1)}, bf16[64,4,64,2...) while((s32[]{:T(128)}, f32[4,64,2,6]{1,2,3,0:T(2,128)S(1)}, ...), condition=%wide.region_4.5_spmd, body=%wide.region_3.4_spmd.sunk | while | flops 1597445 | bytes 4354199 | solution.py:37
  378.6 2.5 fusion.101
  382.3 2.5 fusion.101
  386.1 2.5 fusion.101
  389.8 2.5 fusion.101
  393.5 2.5 fusion.101
  397.2 2.5 fusion.101
  400.9 2.5 fusion.101
  404.6 2.5 fusion.101
  408.3 2.5 fusion.101
  412.0 2.5 fusion.101
  415.7 2.5 fusion.101
  419.5 2.5 fusion.101
  423.2 2.5 fusion.101
  426.9 2.5 fusion.101
  430.6 2.5 fusion.101
  434.3 2.5 fusion.101
  438.0 2.5 fusion.101
  441.7 2.5 fusion.101
  445.4 2.5 fusion.101
  449.2 2.5 fusion.101
  452.9 2.5 fusion.101
  456.6 2.5 fusion.101
  460.3 2.5 fusion.101
  464.0 2.5 fusion.101
  467.7 2.5 fusion.101
  471.4 2.5 fusion.101
  475.1 2.5 fusion.101
  478.8 2.5 fusion.101
  482.6 2.5 fusion.101
  486.3 2.5 fusion.101
  490.0 2.5 fusion.101
  493.7 2.5 fusion.101
  497.4 2.5 fusion.101
  501.1 2.5 fusion.101
  541.9 2.5 fusion.101
  612.3 3.2 multiply_reduce_fusion.1
  617.9 96.3 %all-gather.9.cloned.1.call-done = bf16[512,1,1536]{2,1,0:T(2,128)(2,1)} async-done(((bf16[4,1,1536]{2,1,0:T(2,128)(2,1)}), bf16[512,1,1536]{2,1,0:T(2,128)(2,1)}) %all-gather.9.cloned.1.call-update) | async-done | bytes 1572880 | tf_op jit(solution)/shard_map/all_gather | solution.py:174
  722.4 3.3 fusion.38
  725.7 150.3 %all-reduce.3.cloned.1.call-done = f32[512,1536]{1,0:T(8,128)} async-done(((f32[512,1536]{1,0:T(8,128)}), f32[512,1536]{1,0:T(8,128)}) %all-reduce.3.cloned.1.call-update) | async-done | bytes 3145744
  (329 shorter events, 171.7 us)
Async XLA Ops:
  6.5 713.7 %copy-start = (bf16[192,1536]{1,0:T(8,128)(2,1)S(1)}, bf16[192,1536]{1,0:T(8,128)(2,1)}, u32[]{:S(2)}) copy-start(bf16[192,1536]{1,0:T(8,128)(2,1)} %param.28) | copy-start | bytes 1769476
  8.1 3.8 copy-start.9
  11.9 15.2 %copy-start.1 = (bf16[64,64,256]{2,1,0:T(8,128)(2,1)S(1)}, bf16[64,64,256]{2,1,0:T(8,128)(2,1)}, u32[]{:S(2)}) copy-start(bf16[64,64,256]{2,1,0:T(8,128)(2,1)} %param.18) | copy-start | bytes 6291460
  14.6 26.9 %all-to-all-start = ((bf16[4,64,1536]{2,0,1:T(4,128)(2,1)}), bf16[4,64,1536]{2,0,1:T(4,128)(2,1)S(1)}, u32[]{:S(2)}, u32[]{:S(2)}) async-start(bf16[4,64,1536]{2,0,1:T(4,128)(2,1)} %tile.2), calls=%async_computation | async-start | bytes 1572864 | tf_op jit(solution)/shard_map/all_to_all | solution.py:20
  26.6 349.2 %all-gather.7.cloned.1.call-start = ((), (), s32[]{:S(2)}) async-start(), calls=%async_computation.1 | async-start | bytes 68157440 | tf_op jit(solution)/shard_map/all_gather | solution.py:25
  29.2 4.1 copy-start.10
  43.0 3.4 copy-start.2
  46.4 2.2 copy-start.12
  46.5 2.3 copy-start.8
  48.6 665.6 %all-gather.9.cloned.1.call-start = ((), (), s32[]{:S(2)}) async-start(), calls=%async_computation.2 | async-start | bytes 3170304 | tf_op jit(solution)/shard_map/all_gather | solution.py:174
  202.7 155.0 %copy-start.3 = (bf16[256,64,2,6]{1,2,3,0:T(2,128)(2,1)}, bf16[256,64,2,6]{1,2,3,0:T(2,128)(2,1)S(1)}, u32[]{:S(2)}) copy-start(bf16[256,64,2,6]{1,2,3,0:T(2,128)(2,1)S(1)} %all-gather) | copy-start | bytes 1179652
  357.7 0.9 copy-start.4
  377.4 234.8 %copy-start.6 = (bf16[4,1,1536]{2,0,1:T(4,128)(2,1)S(1)}, bf16[4,1,1536]{2,0,1:T(4,128)(2,1)}, u32[]{:S(2)}) copy-start(bf16[4,1,1536]{2,0,1:T(4,128)(2,1)} %param.16) | copy-start | bytes 36868
  612.2 4.2 copy-start.7
  612.3 102.0 %copy-start.11 = (bf16[1536,32]{0,1:T(8,128)(2,1)S(1)}, bf16[1536,32]{0,1:T(8,128)(2,1)}, u32[]{:S(2)}) copy-start(bf16[1536,32]{0,1:T(8,128)(2,1)} %param.25) | copy-start | bytes 294916
  616.2 259.8 %all-reduce.3.cloned.1.call-start = ((), (), s32[]{:S(2)}) async-start(), calls=%async_computation.3 | async-start | bytes 6291456
  716.7 3.1 copy-start.5
Sparse Core Ops, SparseCore 0:
  48.7 327.0 all-gather.6
  616.3 97.8 all-gather.8
  725.9 150.1 all-reduce.2
